TPU v7x, 256 devices: a whole 4x4x8 slice. The times are simulated.
256 devices in a mesh: section: 8 (over y_lo, x), expert: 32 (over z, y_hi, core).
Axes of the slice: x: 4, y: 4 (y_hi: 2, y_lo: 2; y = y_hi * 2 + y_lo), z: 8, core: 2. Of those that a mesh axis runs over, the one named last changes fastest.
Arguments:
- tokens: bfloat16 [32768, 4096], P(('section', 'expert')), may hold values from -6 to 6
- expert_ids: int32 [32768], P(('section', 'expert')), may hold values from 0 to 31, as said below
- slot_ids: int32 [32768], P(('section', 'expert')), may hold values from 0 to 4, as said below
- router: bfloat16 [4096, 32], replicated, may hold values from -0.09375 to 0.09375
- w_in: bfloat16 [32, 4096, 5120], P('expert', None, 'section'), may hold values from -0.09375 to 0.09375
- w_out: bfloat16 [32, 5120, 4096], P('expert', 'section'), may hold values from -0.078125 to 0.078125
Outputs:
- moe_out: bfloat16 [32768, 4096], P(('section', 'expert'))
Inputs may be any that keep to these rules, and one draw needn't show every extreme that they name: `expert_ids`: within each aligned block of 128 rows (the tokens of one device) no pair of expert id and slot position occurs twice, so each expert receives at most 5 tokens from one device. `slot_ids`: a token's position among the 5 slots that its device keeps for its expert.
All inputs are finite; a program needn't handle non-finite values.
Results may differ from a plain program's by a relative error of at most 0.018.
Values may be sent and summed in bfloat16 or wider, within the bound.
No kernel may reach another device: no remote copies, remote signals or barrier semaphores. Data moves between devices by JAX's collectives and lax.ppermute only.
A program may use at most 128 MiB of HBM per device.

v0:
```python
import jax
import jax.numpy as jnp
from jax import lax
from jax.sharding import PartitionSpec as P


def per_device(tokens, expert_ids, slot_ids, router, w_in, w_out):
    tok_rows, width_model = tokens.shape
    experts = router.shape[1]
    capacity = 5 * tok_rows // (4 * experts)
    cell_index = expert_ids * capacity + slot_ids
    onehot = (
        cell_index[None, :] == jnp.arange(experts * capacity, dtype=jnp.int32)[:, None]
    ).astype(jnp.bfloat16)
    dispatch = jnp.dot(onehot, tokens, preferred_element_type=jnp.float32).astype(jnp.bfloat16)
    dispatch = dispatch.reshape(1, experts, capacity, width_model)
    inward = w_in[0]
    outward = w_out[0]
    grouped = lax.all_gather(dispatch, "section", axis=0, tiled=True)
    arrived = lax.all_to_all(grouped, "expert", split_axis=1, concat_axis=1, tiled=True)
    flat = arrived.reshape(-1, width_model)
    hidden = jax.nn.relu(jnp.dot(flat, inward, preferred_element_type=jnp.float32)).astype(
        jnp.bfloat16
    )
    summed = lax.psum_scatter(
        jnp.dot(hidden, outward, preferred_element_type=jnp.float32).astype(jnp.bfloat16),
        "section",
        scatter_dimension=0,
        tiled=True,
    )
    expert_out = summed.reshape(experts, capacity, width_model)
    returned = lax.all_to_all(expert_out, "expert", split_axis=0, concat_axis=0, tiled=True)
    combined = lax.dot_general(
        onehot,
        returned.reshape(-1, width_model),
        (((0,), (0,)), ((), ())),
        preferred_element_type=jnp.float32,
    )
    logits = jnp.dot(tokens, router, preferred_element_type=jnp.float32)
    chosen = expert_ids[:, None] == jnp.arange(experts, dtype=jnp.int32)[None, :]
    gating = jax.nn.sigmoid(jnp.sum(jnp.where(chosen, logits, jnp.zeros_like(logits)), axis=1))
    return (gating[:, None] * combined).astype(jnp.bfloat16)


def solution(mesh):
    return jax.shard_map(
        per_device,
        mesh=mesh,
        in_specs=(
            P(("section", "expert"), None),
            P(("section", "expert")),
            P(("section", "expert")),
            P(),
            P("expert", None, "section"),
            P("expert", "section", None),
        ),
        out_specs=P(("section", "expert"), None),
        check_vma=False,
    )
```

profile of v0, /device:TPU:1, one launch (start us, length us, event | category | flops | bytes accessed | tf_op | source)
XLA Modules:
  0.0 630.1 jit_solution(9197665170791650322)
XLA Ops:
  6.5 0.0 copy-start
  6.5 0.0 all-gather.2.cloned.1.call-start
  6.5 0.8 multiply_add_fusion
  7.3 0.5 copy-done
  7.8 1.6 convolution_convert_fusion.1
  9.4 1.6 reshape.20
  11.0 1.9 copy.7
  13.0 0.0 all-gather.2.cloned.1.call-update
  13.0 0.0 reduce-scatter.2.cloned.1.call-start
  13.0 118.0 %all-gather.2.cloned.1.call-done = bf16[8,32,5,4096]{3,1,2,0:T(8,128)(2,1)} async-done(((bf16[1,32,5,4096]{3,1,2,0:T(8,128)(2,1)}), bf16[8,32,5,4096]{3,1,2,0:T(8,128)(2,1)}) %all-gather.2.cloned.1.call-update) | async-done | bytes 10485776 | tf_op jit(solution)/shard_map/all_gather | solution.py:19
  131.0 13.5 %copy.8 = bf16[8,32,5,4096]{3,0,2,1:T(8,128)(2,1)} copy(bf16[8,32,5,4096]{3,1,2,0:T(8,128)(2,1)} %all-gather.2.cloned.1.call-done) | data formatting | bytes 20971520 | tf_op jit(solution)/shard_map/all_gather | solution.py:19
  144.6 240.2 %all_to_all.10 = bf16[8,32,5,4096]{3,0,2,1:T(8,128)(2,1)S(1)} all-to-all(bf16[8,32,5,4096]{3,0,2,1:T(8,128)(2,1)} %copy.8), channel_id=1, replica_groups=mesh['section'=8,'expert'=32] {'expert'}, dimensions={1} | all-to-all | bytes 20971520 | tf_op jit(solution)/shard_map/all_to_all | solution.py:20
  384.8 21.2 %copy.9 = bf16[8,32,5,4096]{3,2,1,0:T(8,128)(2,1)} copy(bf16[8,32,5,4096]{3,0,2,1:T(8,128)(2,1)S(1)} %all_to_all.10) | data formatting | bytes 20971520 | tf_op jit(solution)/shard_map/all_to_all | solution.py:20
  406.0 0.0 slice-start
  406.0 16.9 %reshape.21 = bf16[1280,4096]{1,0:T(8,128)(2,1)} reshape(bf16[8,32,5,4096]{3,2,1,0:T(8,128)(2,1)} %copy.9) | data formatting | bytes 20971520 | tf_op jit(solution)/shard_map/reshape | solution.py:21
  423.0 0.0 slice-start.1
  423.0 12.6 %fusion.7 = bf16[1280,640]{1,0:T(8,128)(2,1)S(1)} fusion(bf16[1280,4096]{1,0:T(8,128)(2,1)} %reshape.21, bf16[1,4096,640]{2,1,0:T(8,128)(2,1)} %param.10), kind=kOutput, calls=%fused_computation.8 | convolution fusion | flops 6712524800 | bytes 17367040 | tf_op jit(solution)/shard_map/dot_general | solution.py:22
  435.6 0.0 slice-done
  435.6 0.0 slice-done.1
  435.7 10.7 %convolution_convert_fusion = bf16[1280,4096]{1,0:T(8,128)(2,1)} fusion(bf16[1280,640]{1,0:T(8,128)(2,1)S(1)} %fusion.7, bf16[1,640,4096]{2,1,0:T(8,128)(2,1)S(1)} %bitcast.17), kind=kOutput, calls=%fused_computation | convolution fusion | flops 6716129280 | bytes 17367040 | tf_op jit(solution)/shard_map/dot_general | solution.py:26
  446.3 0.0 reduce-scatter.2.cloned.1.call-update
  446.4 0.0 copy-start.1
  446.4 0.0 copy-start.2
  446.4 110.0 %reduce-scatter.2.cloned.1.call-done = bf16[160,4096]{1,0:T(8,128)(2,1)} async-done(((bf16[1280,4096]{1,0:T(8,128)(2,1)}), bf16[160,4096]{1,0:T(8,128)(2,1)}) %reduce-scatter.2.cloned.1.call-update) | async-done | bytes 1310736 | tf_op jit(solution)/shard_map/reduce_scatter | solution.py:25
  556.4 2.7 reshape.22
  559.1 9.9 %all-to-all-start.1 = ((bf16[32,5,4096]{2,1,0:T(8,128)(2,1)}), bf16[32,5,4096]{2,1,0:T(8,128)(2,1)S(1)}, u32[]{:S(2)}, u32[]{:S(2)}) async-start(bf16[32,5,4096]{2,1,0:T(8,128)(2,1)} %reshape.22), calls=%async_computation.2 | async-start | bytes 4194304 | tf_op jit(solution)/shard_map/all_to_all | solution.py:32
  569.0 0.0 copy-done.1
  569.0 0.0 copy-done.2
  569.0 0.5 fusion.10
  569.5 49.6 %all-to-all-done.1 = bf16[32,5,4096]{2,1,0:T(8,128)(2,1)S(1)} async-done(((bf16[32,5,4096]{2,1,0:T(8,128)(2,1)}), bf16[32,5,4096]{2,1,0:T(8,128)(2,1)S(1)}, u32[]{:S(2)}, u32[]{:S(2)}) %all-to-all-start.1) | async-done | bytes 1310752 | tf_op jit(solution)/shard_map/all_to_all | solution.py:32
  619.1 1.4 reshape.23
  620.5 2.8 fusion.3
  (2 shorter events, 0.0 us)
Async XLA Ops:
  6.5 1.3 copy-start
  6.5 124.5 %all-gather.2.cloned.1.call-start = ((), (), s32[]{:S(2)}) async-start(), calls=%async_computation.3 | async-start | bytes 11796480 | tf_op jit(solution)/shard_map/all_gather | solution.py:19
  13.0 543.4 %reduce-scatter.2.cloned.1.call-start = ((), (), s32[]{:S(2)}) async-start(), calls=%async_computation.4 | async-start | bytes 11796480 | tf_op jit(solution)/shard_map/reduce_scatter | solution.py:25
  406.0 29.6 %slice-start = ((s8[5242880]{0:T(1024)(128)(4,1)}), s8[1048576]{0:T(1024)(128)(4,1)S(1)}, s32[]{:S(2)}) async-start(s8[5242880]{0:T(1024)(128)(4,1)} %bitcast.16), calls=%async_computation.5 | async-start | bytes 2097152
  423.0 12.7 %slice-start.1 = ((s8[5242880]{0:T(1024)(128)(4,1)}), s8[4194304]{0:T(1024)(128)(4,1)S(1)}, s32[]{:S(2)}) async-start(s8[5242880]{0:T(1024)(128)(4,1)} %bitcast.16), calls=%async_computation.6 | async-start | bytes 8388608
  446.4 122.6 %copy-start.1 = (bf16[4096,32]{0,1:T(8,128)(2,1)S(1)}, bf16[4096,32]{0,1:T(8,128)(2,1)}, u32[]{:S(2)}) copy-start(bf16[4096,32]{0,1:T(8,128)(2,1)} %param.9) | copy-start | bytes 786436
  446.4 122.6 %copy-start.2 = (s32[128]{0:T(128)S(1)}, s32[128]{0:T(128)}, u32[]{:S(2)}) copy-start(s32[128]{0:T(128)} %param.7) | copy-start | bytes 1540
  559.1 60.0 %all-to-all-start.1 = ((bf16[32,5,4096]{2,1,0:T(8,128)(2,1)}), bf16[32,5,4096]{2,1,0:T(8,128)(2,1)S(1)}, u32[]{:S(2)}, u32[]{:S(2)}) async-start(bf16[32,5,4096]{2,1,0:T(8,128)(2,1)} %reshape.22), calls=%async_computation.2 | async-start | bytes 4194304 | tf_op jit(solution)/shard_map/all_to_all | solution.py:32
Sparse Core Ops, SparseCore 0:
  13.1 117.8 all-gather.1
  446.5 109.8 reduce-scatter.1
where the time goes:
time: 631 us; the launch traced here: 630 us
  waiting for transfers between devices  278 us (44%)
  blocking collectives  240 us (38%)
  local copies, waits for them, and re-layouts  59.9 us (9%)
  matrix products  28.2 us (4%)
  between operations  13.5 us (2%)
  starting transfers between devices  9.99 us (2%)
    all_to_all x1, blocking collectives, per_device(): lax.all_to_all(grouped, 'expert', split_axis=1, concat_axis=1, tiled=True)  240 us
    all_gather x1, waiting for transfers between devices, per_device(): grouped = lax.all_gather(dispatch, 'section', axis=0, tiled=True)  118 us
    reduce_scatter x1, waiting for transfers between devices, per_device(): lax.psum_scatter(jnp.dot(hidden, outward, preferred_element_type=jnp.floa...  110 us
    all_to_all x1, waiting for transfers between devices, per_device(): lax.all_to_all(expert_out, 'expert', split_axis=0, concat_axis=0, tiled=T...  49.6 us
    all_to_all x1, local copies, waits for them, and re-layouts, per_device(): lax.all_to_all(grouped, 'expert', split_axis=1, concat_axis=1, tiled=True)  21.2 us
    reshape x1, local copies, waits for them, and re-layouts, per_device(): flat = arrived.reshape(-1, width_model)  16.9 us
    all_gather x1, local copies, waits for them, and re-layouts, per_device(): grouped = lax.all_gather(dispatch, 'section', axis=0, tiled=True)  13.5 us
    dot_general x1, matrix products, per_device(): jnp.dot(flat, inward, preferred_element_type=jnp.float32)  12.6 us
  transfers between devices with their start and end apart: 3, of which 3 were waited for; matrix products, arithmetic and copies ran while one was open for 0% of the time, Pallas kernels for 0%

commit v1 on v0

--- a/solution.py
+++ b/solution.py
@@ -16,8 +16,8 @@
     dispatch = dispatch.reshape(1, experts, capacity, width_model)
     inward = w_in[0]
     outward = w_out[0]
-    grouped = lax.all_gather(dispatch, "section", axis=0, tiled=True)
-    arrived = lax.all_to_all(grouped, "expert", split_axis=1, concat_axis=1, tiled=True)
+    routed = lax.all_to_all(dispatch[0], "expert", split_axis=0, concat_axis=0, tiled=True)
+    arrived = lax.all_gather(routed, "section", axis=0, tiled=True)
     flat = arrived.reshape(-1, width_model)
     hidden = jax.nn.relu(jnp.dot(flat, inward, preferred_element_type=jnp.float32)).astype(
         jnp.bfloat16

time: 631 us -> 432 us (0.68)
  blocking collectives: 240 us -> 63.2 us
  local copies, waits for them, and re-layouts: 59.9 us -> 40.3 us
    all_to_all x1, blocking collectives: 240 us -> 63.2 us  [per_device(): lax.all_to_all(dispatch[0], 'expert', split_axis=0, concat_axis=0, tiled=...]
    all_to_all x1, local copies, waits for them, and re-layouts: 21.2 us -> 1.94 us  [per_device(): lax.all_to_all(dispatch[0], 'expert', split_axis=0, concat_axis=0, tiled=...]
    all_gather x1, waiting for transfers between devices: 118 us -> 111 us  [per_device(): arrived = lax.all_gather(routed, 'section', axis=0, tiled=True)]
where the time goes in v1:
time: 432 us; the launch traced here: 431 us
  waiting for transfers between devices  275 us (64%)
  blocking collectives  63.2 us (15%)
  local copies, waits for them, and re-layouts  40.3 us (9%)
  matrix products  28.2 us (7%)
  between operations  13.5 us (3%)
  starting transfers between devices  10.1 us (2%)
    reduce_scatter x1, waiting for transfers between devices, per_device(): lax.psum_scatter(jnp.dot(hidden, outward, preferred_element_type=jnp.floa...  114 us
    all_gather x1, waiting for transfers between devices, per_device(): arrived = lax.all_gather(routed, 'section', axis=0, tiled=True)  111 us
    all_to_all x1, blocking collectives, per_device(): lax.all_to_all(dispatch[0], 'expert', split_axis=0, concat_axis=0, tiled=...  63.2 us
    all_to_all x1, waiting for transfers between devices, per_device(): lax.all_to_all(expert_out, 'expert', split_axis=0, concat_axis=0, tiled=T...  49.6 us
    reshape x1, local copies, waits for them, and re-layouts, per_device(): flat = arrived.reshape(-1, width_model)  16.9 us
    all_gather x1, local copies, waits for them, and re-layouts, per_device(): arrived = lax.all_gather(routed, 'section', axis=0, tiled=True)  15.2 us
    dot_general x1, matrix products, per_device(): jnp.dot(flat, inward, preferred_element_type=jnp.float32)  12.6 us
    dot_general x1, matrix products, per_device(): jnp.dot(hidden, outward, preferred_element_type=jnp.float32)  10.7 us
  transfers between devices with their start and end apart: 3, of which 3 were waited for; matrix products, arithmetic and copies ran while one was open for 0% of the time, Pallas kernels for 0%

profile of v1, /device:TPU:1, one launch (start us, length us, event | category | flops | bytes accessed | tf_op | source)
XLA Modules:
  0.0 430.7 jit_solution(12639602397897531494)
XLA Ops:
  6.5 0.0 copy-start
  6.5 0.0 all-gather.2.cloned.1.call-start
  6.5 0.8 multiply_add_fusion
  7.3 0.5 copy-done
  7.8 1.6 convolution_convert_fusion.1
  9.4 1.6 squeeze_reshape.3
  11.0 63.2 %all_to_all.10 = bf16[32,5,4096]{2,1,0:T(8,128)(2,1)S(1)} all-to-all(bf16[32,5,4096]{2,1,0:T(8,128)(2,1)S(1)} %squeeze_reshape.3), channel_id=1, replica_groups=mesh['section'=8,'expert'=32] {'expert'}, dimensions={0} | all-to-all | bytes 2621440 | tf_op jit(solution)/shard_map/all_to_all | solution.py:19
  74.2 1.9 copy.7
  76.1 0.0 all-gather.2.cloned.1.call-update
  76.1 0.0 reduce-scatter.2.cloned.1.call-start
  76.2 111.0 %all-gather.2.cloned.1.call-done = bf16[256,5,4096]{2,0,1:T(8,128)(2,1)} async-done(((bf16[32,5,4096]{2,0,1:T(8,128)(2,1)}), bf16[256,5,4096]{2,0,1:T(8,128)(2,1)}) %all-gather.2.cloned.1.call-update) | async-done | bytes 10485776 | tf_op jit(solution)/shard_map/all_gather | solution.py:20
  187.2 15.2 %copy.8 = bf16[256,5,4096]{2,1,0:T(8,128)(2,1)} copy(bf16[256,5,4096]{2,0,1:T(8,128)(2,1)} %all-gather.2.cloned.1.call-done) | data formatting | bytes 20971520 | tf_op jit(solution)/shard_map/all_gather | solution.py:20
  202.4 0.0 slice-start
  202.4 16.9 %reshape.17 = bf16[1280,4096]{1,0:T(8,128)(2,1)} reshape(bf16[256,5,4096]{2,1,0:T(8,128)(2,1)} %copy.8) | data formatting | bytes 20971520 | tf_op jit(solution)/shard_map/reshape | solution.py:21
  219.4 0.0 slice-start.1
  219.4 12.6 %fusion.7 = bf16[1280,640]{1,0:T(8,128)(2,1)S(1)} fusion(bf16[1280,4096]{1,0:T(8,128)(2,1)} %reshape.17, bf16[1,4096,640]{2,1,0:T(8,128)(2,1)} %param.10), kind=kOutput, calls=%fused_computation.8 | convolution fusion | flops 6712524800 | bytes 17367040 | tf_op jit(solution)/shard_map/dot_general | solution.py:22
  232.0 0.0 slice-done
  232.0 0.0 slice-done.1
  232.0 10.7 %convolution_convert_fusion = bf16[1280,4096]{1,0:T(8,128)(2,1)} fusion(bf16[1280,640]{1,0:T(8,128)(2,1)S(1)} %fusion.7, bf16[1,640,4096]{2,1,0:T(8,128)(2,1)S(1)} %bitcast.17), kind=kOutput, calls=%fused_computation | convolution fusion | flops 6716129280 | bytes 17367040 | tf_op jit(solution)/shard_map/dot_general | solution.py:26
  242.7 0.0 reduce-scatter.2.cloned.1.call-update
  242.8 114.1 %reduce-scatter.2.cloned.1.call-done = bf16[160,4096]{1,0:T(8,128)(2,1)} async-done(((bf16[1280,4096]{1,0:T(8,128)(2,1)}), bf16[160,4096]{1,0:T(8,128)(2,1)}) %reduce-scatter.2.cloned.1.call-update) | async-done | bytes 1310736 | tf_op jit(solution)/shard_map/reduce_scatter | solution.py:25
  356.8 2.7 reshape.18
  359.5 0.0 copy-start.1
  359.5 0.0 copy-start.2
  359.5 10.1 %all-to-all-start.1 = ((bf16[32,5,4096]{2,1,0:T(8,128)(2,1)}), bf16[32,5,4096]{2,1,0:T(8,128)(2,1)S(1)}, u32[]{:S(2)}, u32[]{:S(2)}) async-start(bf16[32,5,4096]{2,1,0:T(8,128)(2,1)} %reshape.18), calls=%async_computation.2 | async-start | bytes 4194304 | tf_op jit(solution)/shard_map/all_to_all | solution.py:32
  369.6 0.0 copy-done.1
  369.6 0.0 copy-done.2
  369.6 0.5 fusion.10
  370.1 49.6 %all-to-all-done.1 = bf16[32,5,4096]{2,1,0:T(8,128)(2,1)S(1)} async-done(((bf16[32,5,4096]{2,1,0:T(8,128)(2,1)}), bf16[32,5,4096]{2,1,0:T(8,128)(2,1)S(1)}, u32[]{:S(2)}, u32[]{:S(2)}) %all-to-all-start.1) | async-done | bytes 1310752 | tf_op jit(solution)/shard_map/all_to_all | solution.py:32
  419.7 1.4 reshape.19
  421.1 2.8 fusion.3
  (2 shorter events, 0.0 us)
Async XLA Ops:
  6.5 1.3 copy-start
  6.5 180.7 %all-gather.2.cloned.1.call-start = ((), (), s32[]{:S(2)}) async-start(), calls=%async_computation.3 | async-start | bytes 11796480 | tf_op jit(solution)/shard_map/all_gather | solution.py:20
  76.1 280.7 %reduce-scatter.2.cloned.1.call-start = ((), (), s32[]{:S(2)}) async-start(), calls=%async_computation.4 | async-start | bytes 11796480 | tf_op jit(solution)/shard_map/reduce_scatter | solution.py:25
  202.4 29.6 %slice-start = ((s8[5242880]{0:T(1024)(128)(4,1)}), s8[1048576]{0:T(1024)(128)(4,1)S(1)}, s32[]{:S(2)}) async-start(s8[5242880]{0:T(1024)(128)(4,1)} %bitcast.16), calls=%async_computation.5 | async-start | bytes 2097152
  219.4 12.7 %slice-start.1 = ((s8[5242880]{0:T(1024)(128)(4,1)}), s8[4194304]{0:T(1024)(128)(4,1)S(1)}, s32[]{:S(2)}) async-start(s8[5242880]{0:T(1024)(128)(4,1)} %bitcast.16), calls=%async_computation.6 | async-start | bytes 8388608
  359.5 10.1 %copy-start.1 = (bf16[4096,32]{0,1:T(8,128)(2,1)S(1)}, bf16[4096,32]{0,1:T(8,128)(2,1)}, u32[]{:S(2)}) copy-start(bf16[4096,32]{0,1:T(8,128)(2,1)} %param.9) | copy-start | bytes 786436
  359.5 10.1 %copy-start.2 = (s32[128]{0:T(128)S(1)}, s32[128]{0:T(128)}, u32[]{:S(2)}) copy-start(s32[128]{0:T(128)} %param.7) | copy-start | bytes 1540
  359.5 60.2 %all-to-all-start.1 = ((bf16[32,5,4096]{2,1,0:T(8,128)(2,1)}), bf16[32,5,4096]{2,1,0:T(8,128)(2,1)S(1)}, u32[]{:S(2)}, u32[]{:S(2)}) async-start(bf16[32,5,4096]{2,1,0:T(8,128)(2,1)} %reshape.18), calls=%async_computation.2 | async-start | bytes 4194304 | tf_op jit(solution)/shard_map/all_to_all | solution.py:32
Sparse Core Ops, SparseCore 0:
  76.3 110.8 all-gather.1
  242.9 113.9 reduce-scatter.1

commit v2 on v1

v2 whole, which is shorter than its diff:
```python
import jax
import jax.numpy as jnp
from jax import lax
from jax.sharding import PartitionSpec as P

CHUNK_SLOTS = (1, 1, 1, 1, 1)


def per_device(tokens, expert_ids, slot_ids, router, w_in, w_out):
    tok_rows, width_model = tokens.shape
    experts = router.shape[1]
    capacity = 5 * tok_rows // (4 * experts)
    assert sum(CHUNK_SLOTS) == capacity
    cell_index = slot_ids * experts + expert_ids
    onehot = (
        cell_index[None, :] == jnp.arange(experts * capacity, dtype=jnp.int32)[:, None]
    ).astype(jnp.bfloat16)
    dispatch = jnp.dot(onehot, tokens, preferred_element_type=jnp.float32).astype(jnp.bfloat16)
    inward = w_in[0]
    outward = w_out[0]

    combined = None
    start = 0
    for slots in CHUNK_SLOTS:
        rows = slice(start * experts, (start + slots) * experts)
        start += slots
        part = dispatch[rows].reshape(slots, experts, width_model)
        routed = lax.all_to_all(part, "expert", split_axis=1, concat_axis=1, tiled=True)
        arrived = lax.all_gather(
            routed.reshape(-1, width_model), "section", axis=0, tiled=True
        )
        hidden = jax.nn.relu(
            jnp.dot(arrived, inward, preferred_element_type=jnp.float32)
        ).astype(jnp.bfloat16)
        summed = lax.psum_scatter(
            jnp.dot(hidden, outward, preferred_element_type=jnp.float32).astype(jnp.bfloat16),
            "section",
            scatter_dimension=0,
            tiled=True,
        )
        returned = lax.all_to_all(
            summed.reshape(slots, experts, width_model),
            "expert",
            split_axis=1,
            concat_axis=1,
            tiled=True,
        )
        piece = lax.dot_general(
            onehot[rows],
            returned.reshape(-1, width_model),
            (((0,), (0,)), ((), ())),
            preferred_element_type=jnp.float32,
        )
        combined = piece if combined is None else combined + piece
    logits = jnp.dot(tokens, router, preferred_element_type=jnp.float32)
    chosen = expert_ids[:, None] == jnp.arange(experts, dtype=jnp.int32)[None, :]
    gating = jax.nn.sigmoid(jnp.sum(jnp.where(chosen, logits, jnp.zeros_like(logits)), axis=1))
    return (gating[:, None] * combined).astype(jnp.bfloat16)


def solution(mesh):
    return jax.shard_map(
        per_device,
        mesh=mesh,
        in_specs=(
            P(("section", "expert"), None),
            P(("section", "expert")),
            P(("section", "expert")),
            P(),
            P("expert", None, "section"),
            P("expert", "section", None),
        ),
        out_specs=P(("section", "expert"), None),
        check_vma=False,
    )
```

time: 432 us -> 567 us (1.31); the launches traced: 431 us -> 559 us
  starting transfers between devices: 10.1 us -> 65.6 us
  blocking collectives: 63.2 us -> 95.5 us
  matrix products: 28.2 us -> 59.9 us
  other arithmetic: 0.77 us -> 23.2 us
  local copies, waits for them, and re-layouts: 40.3 us -> 29.6 us
    all_to_all x1 -> x5, starting transfers between devices: 10.1 us -> 64.4 us  [per_device(): lax.all_to_all(summed.reshape(slots, experts, width_model), 'expert', spl...]
    reduce_scatter x1 -> x5, waiting for transfers between devices: 114 us -> 164 us  [per_device(): lax.psum_scatter(jnp.dot(hidden, outward, preferred_element_type=jnp.floa...]
    all_to_all x1 -> x5, blocking collectives: 63.2 us -> 95.5 us  [per_device(): lax.all_to_all(part, 'expert', split_axis=1, concat_axis=1, tiled=True)]
    all_to_all x1 -> x5, waiting for transfers between devices: 49.6 us -> 20.2 us  [per_device(): lax.all_to_all(summed.reshape(slots, experts, width_model), 'expert', spl...]
    all_gather x1 -> x5, waiting for transfers between devices: 111 us -> 86.6 us  [per_device(): lax.all_gather(routed.reshape(-1, width_model), 'section', axis=0, tiled=...]
    unnamed x1 -> x10, other arithmetic: 0.01 us -> 22.4 us
    dot_general x1 -> x5, matrix products: 10.7 us -> 28.4 us  [per_device(): jnp.dot(hidden, outward, preferred_element_type=jnp.float32)]
    all_gather x1 -> x0, local copies, waits for them, and re-layouts: 15.2 us -> none  [per_device(): arrived = lax.all_gather(routed, 'section', axis=0, tiled=True)]
  transfers between devices with their start and end apart: 3 -> 15, of which waited for: 3 -> 10; matrix products, arithmetic and copies ran while one was open for 0% -> 18% of each run, Pallas kernels for 0% -> 0%
where the time goes in v2:
time: 567 us; the launch traced here: 559 us
  waiting for transfers between devices  271 us (48%)
  blocking collectives  95.5 us (17%)
  starting transfers between devices  65.6 us (12%)
  matrix products  59.9 us (11%)
  local copies, waits for them, and re-layouts  29.6 us (5%)
  other arithmetic  23.2 us (4%)
  between operations  14.4 us (3%)
    reduce_scatter x5, waiting for transfers between devices, per_device(): lax.psum_scatter(jnp.dot(hidden, outward, preferred_element_type=jnp.floa...  164 us
    all_to_all x5, blocking collectives, per_device(): lax.all_to_all(part, 'expert', split_axis=1, concat_axis=1, tiled=True)  95.5 us
    all_gather x5, waiting for transfers between devices, per_device(): lax.all_gather(routed.reshape(-1, width_model), 'section', axis=0, tiled=...  86.6 us
    all_to_all x5, starting transfers between devices, per_device(): lax.all_to_all(summed.reshape(slots, experts, width_model), 'expert', spl...  64.4 us
    dot_general x5, matrix products, per_device(): jnp.dot(hidden, outward, preferred_element_type=jnp.float32)  28.4 us
    dot_general x5, matrix products, per_device(): jnp.dot(arrived, inward, preferred_element_type=jnp.float32)  24.7 us
    unnamed x10, other arithmetic  22.4 us
    all_to_all x5, waiting for transfers between devices, per_device(): lax.all_to_all(summed.reshape(slots, experts, width_model), 'expert', spl...  20.2 us
  transfers between devices with their start and end apart: 15, of which 10 were waited for; matrix products, arithmetic and copies ran while one was open for 18% of the time, Pallas kernels for 0%

profile of v2, /device:TPU:1, one launch (start us, length us, event | category | flops | bytes accessed | tf_op | source)
XLA Modules:
  0.0 558.7 jit_solution(11448328133254249794)
XLA Ops:
  12.0 25.5 %all_to_all.50 = bf16[32,2,2048]{2,1,0:T(2,128)(2,1)S(1)} all-to-all(bf16[32,2,2048]{2,1,0:T(2,128)(2,1)S(1)} %reshape.93), channel_id=1, replica_groups=mesh['section'=8,'expert'=32] {'expert'}, dimensions={0} | all-to-all | bytes 524288 | tf_op jit(solution)/shard_map/all_to_all | solution.py:28
  41.8 17.6 %all_to_all.51 = bf16[32,2,2048]{2,1,0:T(2,128)(2,1)S(1)} all-to-all(bf16[32,2,2048]{2,1,0:T(2,128)(2,1)S(1)} %reshape.97), channel_id=1, replica_groups=mesh['section'=8,'expert'=32] {'expert'}, dimensions={0} | all-to-all | bytes 524288 | tf_op jit(solution)/shard_map/all_to_all | solution.py:28
  63.7 17.0 %all_to_all.52 = bf16[32,2,2048]{2,1,0:T(2,128)(2,1)S(1)} all-to-all(bf16[32,2,2048]{2,1,0:T(2,128)(2,1)S(1)} %reshape.101), channel_id=1, replica_groups=mesh['section'=8,'expert'=32] {'expert'}, dimensions={0} | all-to-all | bytes 524288 | tf_op jit(solution)/shard_map/all_to_all | solution.py:28
  85.5 18.6 %all_to_all.53 = bf16[32,2,2048]{2,1,0:T(2,128)(2,1)S(1)} all-to-all(bf16[32,2,2048]{2,1,0:T(2,128)(2,1)S(1)} %reshape.105), channel_id=1, replica_groups=mesh['section'=8,'expert'=32] {'expert'}, dimensions={0} | all-to-all | bytes 524288 | tf_op jit(solution)/shard_map/all_to_all | solution.py:28
  108.4 16.8 %all_to_all.54 = bf16[32,2,2048]{2,1,0:T(2,128)(2,1)S(1)} all-to-all(bf16[32,2,2048]{2,1,0:T(2,128)(2,1)S(1)} %reshape.109), channel_id=1, replica_groups=mesh['section'=8,'expert'=32] {'expert'}, dimensions={0} | all-to-all | bytes 524288 | tf_op jit(solution)/shard_map/all_to_all | solution.py:28
  126.6 4.9 fusion.87
  131.5 5.7 %fusion.20 = bf16[256,4096]{1,0:T(8,128)(2,1)} fusion(bf16[256,640]{1,0:T(8,128)(2,1)S(1)} %fusion.87, bf16[1,640,4096]{2,1,0:T(8,128)(2,1)} %param.11), kind=kOutput, calls=%fused_computation.20 | convolution fusion | flops 1343225856 | bytes 7667712 | tf_op jit(solution)/shard_map/dot_general | solution.py:36
  137.5 5.0 fusion.82
  142.5 5.7 %fusion.23 = bf16[256,4096]{1,0:T(8,128)(2,1)} fusion(bf16[256,640]{1,0:T(8,128)(2,1)S(1)} %fusion.82, bf16[1,640,4096]{2,1,0:T(8,128)(2,1)} %param.11), kind=kOutput, calls=%fused_computation.21 | convolution fusion | flops 1343225856 | bytes 7667712 | tf_op jit(solution)/shard_map/dot_general | solution.py:36
  148.2 18.1 %all-gather.15.cloned.1.call-done = bf16[1,256,4096]{2,1,0:T(8,128)(2,1)} async-done(((bf16[1,32,4096]{2,1,0:T(8,128)(2,1)}), bf16[1,256,4096]{2,1,0:T(8,128)(2,1)}) %all-gather.15.cloned.1.call-update) | async-done | bytes 2097168 | tf_op jit(solution)/shard_map/all_gather | solution.py:29
  166.3 4.9 fusion.77
  171.3 5.7 %fusion.26 = bf16[256,4096]{1,0:T(8,128)(2,1)} fusion(bf16[256,640]{1,0:T(8,128)(2,1)S(1)} %fusion.77, bf16[1,640,4096]{2,1,0:T(8,128)(2,1)} %param.11), kind=kOutput, calls=%fused_computation.22 | convolution fusion | flops 1343225856 | bytes 7667712 | tf_op jit(solution)/shard_map/dot_general | solution.py:36
  177.1 34.3 %all-gather.17.cloned.1.call-done = bf16[1,256,4096]{2,1,0:T(8,128)(2,1)} async-done(((bf16[1,32,4096]{2,1,0:T(8,128)(2,1)}), bf16[1,256,4096]{2,1,0:T(8,128)(2,1)}) %all-gather.17.cloned.1.call-update) | async-done | bytes 2097168 | tf_op jit(solution)/shard_map/all_gather | solution.py:29
  211.4 4.9 fusion.72
  216.3 5.7 %fusion.29 = bf16[256,4096]{1,0:T(8,128)(2,1)} fusion(bf16[256,640]{1,0:T(8,128)(2,1)S(1)} %fusion.72, bf16[1,640,4096]{2,1,0:T(8,128)(2,1)} %param.11), kind=kOutput, calls=%fused_computation.23 | convolution fusion | flops 1343225856 | bytes 7667712 | tf_op jit(solution)/shard_map/dot_general | solution.py:36
  222.2 34.1 %all-gather.19.cloned.1.call-done = bf16[1,256,4096]{2,1,0:T(8,128)(2,1)} async-done(((bf16[1,32,4096]{2,1,0:T(8,128)(2,1)}), bf16[1,256,4096]{2,1,0:T(8,128)(2,1)}) %all-gather.19.cloned.1.call-update) | async-done | bytes 2097168 | tf_op jit(solution)/shard_map/all_gather | solution.py:29
  256.4 4.9 fusion.67
  261.3 5.6 %fusion.32 = bf16[256,4096]{1,0:T(8,128)(2,1)} fusion(bf16[256,640]{1,0:T(8,128)(2,1)S(1)} %fusion.67, bf16[1,640,4096]{2,1,0:T(8,128)(2,1)} %param.11), kind=kOutput, calls=%fused_computation.24 | convolution fusion | flops 1343225856 | bytes 7667712 | tf_op jit(solution)/shard_map/dot_general | solution.py:36
  266.9 36.3 %reduce-scatter.6.cloned.1.call-done = bf16[32,4096]{1,0:T(8,128)(2,1)} async-done(((bf16[256,4096]{1,0:T(8,128)(2,1)}), bf16[32,4096]{1,0:T(8,128)(2,1)}) %reduce-scatter.6.cloned.1.call-update) | async-done | bytes 262160 | tf_op jit(solution)/shard_map/reduce_scatter | solution.py:35
  307.9 15.2 %all-to-all-start.1 = ((bf16[32,2,2048]{2,1,0:T(2,128)(2,1)}), bf16[32,2,2048]{2,1,0:T(2,128)(2,1)S(1)}, u32[]{:S(2)}, u32[]{:S(2)}) async-start(bf16[32,2,2048]{2,1,0:T(2,128)(2,1)} %reshape.95), calls=%async_computation.2 | async-start | bytes 524288 | tf_op jit(solution)/shard_map/all_to_all | solution.py:41
  323.1 28.6 %reduce-scatter.8.cloned.1.call-done = bf16[32,4096]{1,0:T(8,128)(2,1)} async-done(((bf16[256,4096]{1,0:T(8,128)(2,1)}), bf16[32,4096]{1,0:T(8,128)(2,1)}) %reduce-scatter.8.cloned.1.call-update) | async-done | bytes 262160 | tf_op jit(solution)/shard_map/reduce_scatter | solution.py:35
  356.4 15.0 %all-to-all-start.3 = ((bf16[32,2,2048]{2,1,0:T(2,128)(2,1)}), bf16[32,2,2048]{2,1,0:T(2,128)(2,1)S(1)}, u32[]{:S(2)}, u32[]{:S(2)}) async-start(bf16[32,2,2048]{2,1,0:T(2,128)(2,1)} %reshape.99), calls=%async_computation.5 | async-start | bytes 524288 | tf_op jit(solution)/shard_map/all_to_all | solution.py:41
  371.4 28.6 %reduce-scatter.10.cloned.1.call-done = bf16[32,4096]{1,0:T(8,128)(2,1)} async-done(((bf16[256,4096]{1,0:T(8,128)(2,1)}), bf16[32,4096]{1,0:T(8,128)(2,1)}) %reduce-scatter.10.cloned.1.call-update) | async-done | bytes 262160 | tf_op jit(solution)/shard_map/reduce_scatter | solution.py:35
  404.6 14.7 %all-to-all-start.5 = ((bf16[32,2,2048]{2,1,0:T(2,128)(2,1)}), bf16[32,2,2048]{2,1,0:T(2,128)(2,1)S(1)}, u32[]{:S(2)}, u32[]{:S(2)}) async-start(bf16[32,2,2048]{2,1,0:T(2,128)(2,1)} %reshape.103), calls=%async_computation.8 | async-start | bytes 524288 | tf_op jit(solution)/shard_map/all_to_all | solution.py:41
  419.9 28.3 %reduce-scatter.12.cloned.1.call-done = bf16[32,4096]{1,0:T(8,128)(2,1)} async-done(((bf16[256,4096]{1,0:T(8,128)(2,1)}), bf16[32,4096]{1,0:T(8,128)(2,1)}) %reduce-scatter.12.cloned.1.call-update) | async-done | bytes 262160 | tf_op jit(solution)/shard_map/reduce_scatter | solution.py:35
  452.8 41.8 %reduce-scatter.14.cloned.1.call-done = bf16[32,4096]{1,0:T(8,128)(2,1)} async-done(((bf16[256,4096]{1,0:T(8,128)(2,1)}), bf16[32,4096]{1,0:T(8,128)(2,1)}) %reduce-scatter.14.cloned.1.call-update) | async-done | bytes 262160 | tf_op jit(solution)/shard_map/reduce_scatter | solution.py:35
  500.6 14.9 %all-to-all-start.7 = ((bf16[32,2,2048]{2,1,0:T(2,128)(2,1)}), bf16[32,2,2048]{2,1,0:T(2,128)(2,1)S(1)}, u32[]{:S(2)}, u32[]{:S(2)}) async-start(bf16[32,2,2048]{2,1,0:T(2,128)(2,1)} %reshape.107), calls=%async_computation.11 | async-start | bytes 524288 | tf_op jit(solution)/shard_map/all_to_all | solution.py:41
  518.1 10.4 %all-to-all-done.7 = bf16[32,2,2048]{2,1,0:T(2,128)(2,1)S(1)} async-done(((bf16[32,2,2048]{2,1,0:T(2,128)(2,1)}), bf16[32,2,2048]{2,1,0:T(2,128)(2,1)S(1)}, u32[]{:S(2)}, u32[]{:S(2)}) %all-to-all-start.7) | async-done | bytes 262176 | tf_op jit(solution)/shard_map/all_to_all | solution.py:41
  528.4 4.6 all-to-all-start.9
  536.2 9.8 %all-to-all-done.9 = bf16[32,2,2048]{2,1,0:T(2,128)(2,1)} async-done(((bf16[32,2,2048]{2,1,0:T(2,128)(2,1)}), bf16[32,2,2048]{2,1,0:T(2,128)(2,1)}, u32[]{:S(2)}, u32[]{:S(2)}) %all-to-all-start.9) | async-done | bytes 262176 | tf_op jit(solution)/shard_map/all_to_all | solution.py:41
  546.0 2.8 reshape.112
  548.8 2.6 fusion.36
  (90 shorter events, 55.7 us)
Async XLA Ops:
  6.5 1.3 copy-start
  6.5 120.0 %all-gather.11.cloned.1.call-start = ((), (), s32[]{:S(2)}) async-start(), calls=%async_computation.20 | async-start | bytes 2359296 | tf_op jit(solution)/shard_map/all_gather | solution.py:29
  38.8 98.7 %all-gather.13.cloned.1.call-start = ((), (), s32[]{:S(2)}) async-start(), calls=%async_computation.21 | async-start | bytes 2359296 | tf_op jit(solution)/shard_map/all_gather | solution.py:29
  60.7 105.6 %all-gather.15.cloned.1.call-start = ((), (), s32[]{:S(2)}) async-start(), calls=%async_computation.22 | async-start | bytes 2359296 | tf_op jit(solution)/shard_map/all_gather | solution.py:29
  82.0 129.4 %all-gather.17.cloned.1.call-start = ((), (), s32[]{:S(2)}) async-start(), calls=%async_computation.23 | async-start | bytes 2359296 | tf_op jit(solution)/shard_map/all_gather | solution.py:29
  105.3 151.0 %all-gather.19.cloned.1.call-start = ((), (), s32[]{:S(2)}) async-start(), calls=%async_computation.24 | async-start | bytes 2359296 | tf_op jit(solution)/shard_map/all_gather | solution.py:29
  126.5 176.7 %reduce-scatter.6.cloned.1.call-start = ((), (), s32[]{:S(2)}) async-start(), calls=%async_computation.15 | async-start | bytes 2359296 | tf_op jit(solution)/shard_map/reduce_scatter | solution.py:35
  137.2 214.5 %reduce-scatter.8.cloned.1.call-start = ((), (), s32[]{:S(2)}) async-start(), calls=%async_computation.16 | async-start | bytes 2359296 | tf_op jit(solution)/shard_map/reduce_scatter | solution.py:35
  148.2 251.8 %reduce-scatter.10.cloned.1.call-start = ((), (), s32[]{:S(2)}) async-start(), calls=%async_computation.17 | async-start | bytes 2359296 | tf_op jit(solution)/shard_map/reduce_scatter | solution.py:35
  177.0 271.2 %reduce-scatter.12.cloned.1.call-start = ((), (), s32[]{:S(2)}) async-start(), calls=%async_computation.18 | async-start | bytes 2359296 | tf_op jit(solution)/shard_map/reduce_scatter | solution.py:35
  222.0 272.7 %reduce-scatter.14.cloned.1.call-start = ((), (), s32[]{:S(2)}) async-start(), calls=%async_computation.19 | async-start | bytes 2359296 | tf_op jit(solution)/shard_map/reduce_scatter | solution.py:35
  307.9 48.5 %all-to-all-start.1 = ((bf16[32,2,2048]{2,1,0:T(2,128)(2,1)}), bf16[32,2,2048]{2,1,0:T(2,128)(2,1)S(1)}, u32[]{:S(2)}, u32[]{:S(2)}) async-start(bf16[32,2,2048]{2,1,0:T(2,128)(2,1)} %reshape.95), calls=%async_computation.2 | async-start | bytes 524288 | tf_op jit(solution)/shard_map/all_to_all | solution.py:41
  353.2 66.1 %copy-start.3 = (bf16[4096,32]{0,1:T(8,128)(2,1)S(1)}, bf16[4096,32]{0,1:T(8,128)(2,1)}, u32[]{:S(2)}) copy-start(bf16[4096,32]{0,1:T(8,128)(2,1)} %param.9) | copy-start | bytes 786436
  353.2 66.1 %copy-start.4 = (s32[128]{0:T(128)S(1)}, s32[128]{0:T(128)}, u32[]{:S(2)}) copy-start(s32[128]{0:T(128)} %param.7) | copy-start | bytes 1540
  356.4 48.2 %all-to-all-start.3 = ((bf16[32,2,2048]{2,1,0:T(2,128)(2,1)}), bf16[32,2,2048]{2,1,0:T(2,128)(2,1)S(1)}, u32[]{:S(2)}, u32[]{:S(2)}) async-start(bf16[32,2,2048]{2,1,0:T(2,128)(2,1)} %reshape.99), calls=%async_computation.5 | async-start | bytes 524288 | tf_op jit(solution)/shard_map/all_to_all | solution.py:41
  404.6 96.0 %all-to-all-start.5 = ((bf16[32,2,2048]{2,1,0:T(2,128)(2,1)}), bf16[32,2,2048]{2,1,0:T(2,128)(2,1)S(1)}, u32[]{:S(2)}, u32[]{:S(2)}) async-start(bf16[32,2,2048]{2,1,0:T(2,128)(2,1)} %reshape.103), calls=%async_computation.8 | async-start | bytes 524288 | tf_op jit(solution)/shard_map/all_to_all | solution.py:41
  500.6 27.9 %all-to-all-start.7 = ((bf16[32,2,2048]{2,1,0:T(2,128)(2,1)}), bf16[32,2,2048]{2,1,0:T(2,128)(2,1)S(1)}, u32[]{:S(2)}, u32[]{:S(2)}) async-start(bf16[32,2,2048]{2,1,0:T(2,128)(2,1)} %reshape.107), calls=%async_computation.11 | async-start | bytes 524288 | tf_op jit(solution)/shard_map/all_to_all | solution.py:41
  516.5 1.0 copy-start.1
  528.4 17.6 %all-to-all-start.9 = ((bf16[32,2,2048]{2,1,0:T(2,128)(2,1)}), bf16[32,2,2048]{2,1,0:T(2,128)(2,1)}, u32[]{:S(2)}, u32[]{:S(2)}) async-start(bf16[32,2,2048]{2,1,0:T(2,128)(2,1)} %reshape.111), calls=%async_computation.14 | async-start | bytes 524288 | tf_op jit(solution)/shard_map/all_to_all | solution.py:41
  534.0 1.7 copy-start.2
Sparse Core Ops, SparseCore 0:
  38.9 35.7 all-gather.10
  76.5 44.7 all-gather.12
  123.0 43.2 all-gather.14
  168.0 43.3 all-gather.16
  213.0 43.3 all-gather.18
  258.8 44.4 reduce-scatter.5
  305.8 45.8 reduce-scatter.7
  354.2 45.7 reduce-scatter.9
  402.5 45.6 reduce-scatter.11
  450.6 44.0 reduce-scatter.13

commit v3 on v1

v3 whole, which is shorter than its diff:
```python
import jax
import jax.numpy as jnp
from jax import lax
from jax.sharding import PartitionSpec as P


def per_device(tokens, expert_ids, slot_ids, router, w_in, w_out):
    tok_rows, width_model = tokens.shape
    experts = router.shape[1]
    capacity = 5 * tok_rows // (4 * experts)
    expert_hit = expert_ids[None, :] == jnp.arange(experts, dtype=jnp.int32)[:, None]
    onehots = [
        (expert_hit & (slot_ids[None, :] == c)).astype(jnp.bfloat16) for c in range(capacity)
    ]
    dispatch = jnp.concatenate(
        [
            jnp.dot(oh, tokens, preferred_element_type=jnp.float32).astype(jnp.bfloat16)
            for oh in onehots
        ],
        axis=1,
    )
    inward = w_in[0]
    outward = w_out[0]
    routed = lax.all_to_all(dispatch, "expert", split_axis=0, concat_axis=0, tiled=True)
    arrived = lax.all_gather(routed, "section", axis=0, tiled=True)
    outs = []
    for c in range(capacity):
        rows = arrived[:, c * width_model : (c + 1) * width_model]
        hidden = jax.nn.relu(
            jnp.dot(rows, inward, preferred_element_type=jnp.float32)
        ).astype(jnp.bfloat16)
        outs.append(
            jnp.dot(hidden, outward, preferred_element_type=jnp.float32).astype(jnp.bfloat16)
        )
    summed = lax.psum_scatter(
        jnp.concatenate(outs, axis=1), "section", scatter_dimension=0, tiled=True
    )
    returned = lax.all_to_all(summed, "expert", split_axis=0, concat_axis=0, tiled=True)
    combined = None
    for c in range(capacity):
        piece = lax.dot_general(
            onehots[c],
            returned[:, c * width_model : (c + 1) * width_model],
            (((0,), (0,)), ((), ())),
            preferred_element_type=jnp.float32,
        )
        combined = piece if combined is None else combined + piece
    logits = jnp.dot(tokens, router, preferred_element_type=jnp.float32)
    gating = jax.nn.sigmoid(
        jnp.sum(jnp.where(expert_hit.T, logits, jnp.zeros_like(logits)), axis=1)
    )
    return (gating[:, None] * combined).astype(jnp.bfloat16)


def solution(mesh):
    return jax.shard_map(
        per_device,
        mesh=mesh,
        in_specs=(
            P(("section", "expert"), None),
            P(("section", "expert")),
            P(("section", "expert")),
            P(),
            P("expert", None, "section"),
            P("expert", "section", None),
        ),
        out_specs=P(("section", "expert"), None),
        check_vma=False,
    )
```

time: 432 us -> 398 us (0.921)
  local copies, waits for them, and re-layouts: 40.3 us -> 19.5 us
  waiting for transfers between devices: 275 us -> 257 us
  blocking collectives: 63.2 us -> 47.5 us
  matrix products: 28.2 us -> 42.4 us
  other arithmetic: 0.77 us -> 6.69 us
    reshape x3 -> x0, local copies, waits for them, and re-layouts: 21 us -> none  [the longest x1 16.9 us: per_device(): flat = arrived.reshape(-1, width_model)]
    all_to_all x1, waiting for transfers between devices: 49.6 us -> 33.2 us  [per_device(): lax.all_to_all(summed, 'expert', split_axis=0, concat_axis=0, tiled=True)]
    all_to_all x1, blocking collectives: 63.2 us -> 47.5 us  [per_device(): lax.all_to_all(dispatch, 'expert', split_axis=0, concat_axis=0, tiled=True)]
    all_gather x1 -> x0, local copies, waits for them, and re-layouts: 15.2 us -> none  [per_device(): arrived = lax.all_gather(routed, 'section', axis=0, tiled=True)]
    unnamed x10 -> x25, local copies, waits for them, and re-layouts: 0.5 us -> 14.8 us
    dot_general x3 -> x15, matrix products: 17 us -> 25.8 us  [the longest x5 16.2 us: per_device(): jnp.dot(rows, inward, preferred_element_type=jnp.float32)]
    all_to_all x0 -> x2, other arithmetic: none -> 5.94 us  [the longest x1 2.97 us: per_device(): lax.all_to_all(dispatch, 'expert', split_axis=0, concat_axis=0, tiled=True)]
    dot_general x1 -> x5, matrix products: 10.7 us -> 16.2 us  [per_device(): jnp.dot(hidden, outward, preferred_element_type=jnp.float32)]
where the time goes in v3:
time: 398 us; the launch traced here: 397 us
  waiting for transfers between devices  257 us (65%)
  blocking collectives  47.5 us (12%)
  matrix products  42.4 us (11%)
  local copies, waits for them, and re-layouts  19.5 us (5%)
  between operations  13.6 us (3%)
  starting transfers between devices  10.2 us (3%)
  other arithmetic  6.69 us (2%)
    reduce_scatter x1, waiting for transfers between devices, per_device(): lax.psum_scatter(jnp.concatenate(outs, axis=1), 'section', scatter_dimens...  114 us
    all_gather x1, waiting for transfers between devices, per_device(): arrived = lax.all_gather(routed, 'section', axis=0, tiled=True)  110 us
    all_to_all x1, blocking collectives, per_device(): lax.all_to_all(dispatch, 'expert', split_axis=0, concat_axis=0, tiled=True)  47.5 us
    all_to_all x1, waiting for transfers between devices, per_device(): lax.all_to_all(summed, 'expert', split_axis=0, concat_axis=0, tiled=True)  33.2 us
    dot_general x5, matrix products, per_device(): jnp.dot(rows, inward, preferred_element_type=jnp.float32)  16.2 us
    dot_general x5, matrix products, per_device(): jnp.dot(hidden, outward, preferred_element_type=jnp.float32)  16.2 us
    unnamed x25, local copies, waits for them, and re-layouts  14.8 us
    all_to_all x1, starting transfers between devices, per_device(): lax.all_to_all(summed, 'expert', split_axis=0, concat_axis=0, tiled=True)  9.93 us
  transfers between devices with their start and end apart: 3, of which 3 were waited for; matrix products, arithmetic and copies ran while one was open for 0% of the time, Pallas kernels for 0%

profile of v3, /device:TPU:1, one launch (start us, length us, event | category | flops | bytes accessed | tf_op | source)
XLA Modules:
  0.0 397.1 jit_solution(12178060793133279673)
XLA Ops:
  6.5 0.7 broadcast_compare_fusion
  7.3 0.5 copy-done
  7.8 1.7 fusion.56
  9.4 1.6 fusion.55
  11.1 1.0 fusion.54
  12.0 1.0 fusion.53
  13.0 1.0 fusion.52
  14.0 0.5 broadcast.26
  14.5 3.0 reduce
  17.5 1.8 reshape.22
  19.3 47.5 %all_to_all.24 = bf16[32,2,10240]{2,1,0:T(2,128)(2,1)S(1)} all-to-all(bf16[32,2,10240]{2,1,0:T(2,128)(2,1)} %reshape.22), channel_id=1, replica_groups=mesh['section'=8,'expert'=32] {'expert'}, dimensions={0} | all-to-all | bytes 2621440 | tf_op jit(solution)/shard_map/all_to_all | solution.py:24
  66.8 3.7 reshape.23
  70.5 4.2 %copy.10 = bf16[32,1,20480]{2,0,1:T(8,128)(2,1)} copy(bf16[32,1,20480]{2,1,0:T(2,128)(2,1)} %reshape.23) | data formatting | bytes 2621440 | tf_op jit(solution)/shard_map/all_to_all | solution.py:24
  75.0 109.9 %all-gather.3.cloned.1.call-done = bf16[256,1,20480]{2,0,1:T(8,128)(2,1)} async-done(((bf16[32,1,20480]{2,0,1:T(8,128)(2,1)}), bf16[256,1,20480]{2,0,1:T(8,128)(2,1)}) %all-gather.3.cloned.1.call-update) | async-done | bytes 10485776 | tf_op jit(solution)/shard_map/all_gather | solution.py:25
  184.9 5.1 %fusion.87 = bf16[256,640]{1,0:T(8,128)(2,1)S(1)} fusion(bf16[1,4096,640]{2,1,0:T(8,128)(2,1)} %param.10, bf16[256,20480]{1,0:T(8,128)(2,1)} %bitcast.86), kind=kOutput, calls=%fused_computation.57 | convolution fusion | flops 1342504960 | bytes 7667712 | tf_op jit(solution)/shard_map/dot_general | solution.py:30
  190.0 5.6 %fusion.92 = bf16[256,640]{1,0:T(8,128)(2,1)S(1)} fusion(bf16[1,4096,640]{2,1,0:T(8,128)(2,1)} %param.10, bf16[256,20480]{1,0:T(8,128)(2,1)} %bitcast.87), kind=kOutput, calls=%fused_computation.58 | convolution fusion | flops 1342504960 | bytes 7667712 | tf_op jit(solution)/shard_map/dot_general | solution.py:30
  195.6 1.8 fusion.97
  197.5 1.8 fusion.102
  199.4 1.8 fusion.107
  201.2 3.2 fusion.23
  204.4 3.2 fusion.29
  207.6 3.2 fusion.35
  210.8 3.4 fusion.41
  214.2 3.2 fusion.47
  217.4 114.0 %reduce-scatter.2.cloned.1.call-done = bf16[32,20480]{1,0:T(8,128)(2,1)} async-done(((bf16[256,20480]{1,0:T(8,128)(2,1)}), bf16[32,20480]{1,0:T(8,128)(2,1)}) %reduce-scatter.2.cloned.1.call-update) | async-done | bytes 1310736 | tf_op jit(solution)/shard_map/reduce_scatter | solution.py:35
  331.5 3.0 reduce.1
  334.4 1.8 reshape.24
  336.3 9.9 %all-to-all-start.1 = ((bf16[32,2,10240]{2,1,0:T(2,128)(2,1)}), bf16[32,2,10240]{2,1,0:T(2,128)(2,1)S(1)}, u32[]{:S(2)}, u32[]{:S(2)}) async-start(bf16[32,2,10240]{2,1,0:T(2,128)(2,1)} %reshape.24), calls=%async_computation.2 | async-start | bytes 2621440 | tf_op jit(solution)/shard_map/all_to_all | solution.py:38
  346.7 33.2 %all-to-all-done.1 = bf16[32,2,10240]{2,1,0:T(2,128)(2,1)S(1)} async-done(((bf16[32,2,10240]{2,1,0:T(2,128)(2,1)}), bf16[32,2,10240]{2,1,0:T(2,128)(2,1)S(1)}, u32[]{:S(2)}, u32[]{:S(2)}) %all-to-all-start.1) | async-done | bytes 1310752 | tf_op jit(solution)/shard_map/all_to_all | solution.py:38
  379.9 3.7 reshape.25
  383.6 3.2 copy.14
  388.7 1.5 fusion.51
  (32 shorter events, 2.7 us)
Async XLA Ops:
  6.5 1.2 copy-start
  6.5 4.5 %copy-start.2 = (s32[128]{0:T(128)S(1)}, s32[128]{0:T(128)}, u32[]{:S(2)}) copy-start(s32[128]{0:T(128)} %param.7) | copy-start | bytes 1540
  6.5 178.3 %all-gather.3.cloned.1.call-start = ((), (), s32[]{:S(2)}) async-start(), calls=%async_computation.4 | async-start | bytes 11796480 | tf_op jit(solution)/shard_map/all_gather | solution.py:25
  74.7 120.8 %slice-start.3 = ((s8[5242880]{0:T(1024)(128)(4,1)}), s8[1048576]{0:T(1024)(128)(4,1)S(1)}, s32[]{:S(2)}) async-start(s8[5242880]{0:T(1024)(128)(4,1)} %bitcast.93), calls=%async_computation.8 | async-start | bytes 2097152
  74.8 256.7 %reduce-scatter.2.cloned.1.call-start = ((), (), s32[]{:S(2)}) async-start(), calls=%async_computation.3 | async-start | bytes 11796480 | tf_op jit(solution)/shard_map/reduce_scatter | solution.py:35
  184.9 10.7 %slice-start = ((s8[10485760]{0:T(1024)(128)(4,1)}), s8[4194304]{0:T(1024)(128)(4,1)S(1)}, s32[]{:S(2)}) async-start(s8[10485760]{0:T(1024)(128)(4,1)} %bitcast.88), calls=%async_computation.5 | async-start | bytes 8388608
  184.9 10.7 %slice-start.1 = ((s8[10485760]{0:T(1024)(128)(4,1)}), s8[4194304]{0:T(1024)(128)(4,1)S(1)}, s32[]{:S(2)}) async-start(s8[10485760]{0:T(1024)(128)(4,1)} %bitcast.88), calls=%async_computation.6 | async-start | bytes 8388608
  184.9 10.7 %slice-start.4 = ((s8[5242880]{0:T(1024)(128)(4,1)}), s8[4194304]{0:T(1024)(128)(4,1)S(1)}, s32[]{:S(2)}) async-start(s8[5242880]{0:T(1024)(128)(4,1)} %bitcast.93), calls=%async_computation.9 | async-start | bytes 8388608
  189.9 5.7 %slice-start.2 = ((s8[10485760]{0:T(1024)(128)(4,1)}), s8[2097152]{0:T(1024)(128)(4,1)S(1)}, s32[]{:S(2)}) async-start(s8[10485760]{0:T(1024)(128)(4,1)} %bitcast.88), calls=%async_computation.7 | async-start | bytes 4194304
  197.5 3.7 slice-start.5
  199.3 1.9 slice-start.6
  334.4 11.8 %copy-start.1 = (bf16[4096,32]{0,1:T(8,128)(2,1)S(1)}, bf16[4096,32]{0,1:T(8,128)(2,1)}, u32[]{:S(2)}) copy-start(bf16[4096,32]{0,1:T(8,128)(2,1)} %param.9) | copy-start | bytes 786436
  336.3 43.6 %all-to-all-start.1 = ((bf16[32,2,10240]{2,1,0:T(2,128)(2,1)}), bf16[32,2,10240]{2,1,0:T(2,128)(2,1)S(1)}, u32[]{:S(2)}, u32[]{:S(2)}) async-start(bf16[32,2,10240]{2,1,0:T(2,128)(2,1)} %reshape.24), calls=%async_computation.2 | async-start | bytes 2621440 | tf_op jit(solution)/shard_map/all_to_all | solution.py:38
Sparse Core Ops, SparseCore 0:
  74.9 109.9 all-gather.2
  217.5 113.8 reduce-scatter.1

commit v4 on v3

--- a/solution.py
+++ b/solution.py
@@ -4,10 +4,75 @@
 from jax.sharding import PartitionSpec as P
 
 
-def per_device(tokens, expert_ids, slot_ids, router, w_in, w_out):
+def _neighbour_perms(n_sec):
+    row = n_sec // 2
+    right = [(s, (s // row) * row + (s % row + 1) % row) for s in range(n_sec)]
+    left = [(s, (s // row) * row + (s % row - 1) % row) for s in range(n_sec)]
+    partner = [(s, (s + row) % n_sec) for s in range(n_sec)]
+    return right, left, partner
+
+
+def _halves(a):
+    h = a.shape[0] // 2
+    return a[:h], a[h:]
+
+
+def _section_gather(mine, perms):
+    right, left, partner = perms
+    pp = lambda v, p: lax.ppermute(v, "section", p)
+    b = pp(mine, right)
+    c = pp(mine, left)
+    a = pp(mine, partner)
+    ap, aq = _halves(a)
+    bp, _ = _halves(b)
+    _, cq = _halves(c)
+    from_left = pp(jnp.concatenate([aq, bp]), right)
+    from_right = pp(jnp.concatenate([ap, cq]), left)
+    from_partner = pp(jnp.concatenate([bp, cq]), partner)
+    h = mine.shape[0] // 2
+    lbar = jnp.concatenate([from_partner[:h], from_left[:h]])
+    rbar = jnp.concatenate([from_right[:h], from_partner[h:]])
+    far = jnp.concatenate([from_left[h:], from_right[h:]])
+    farbar = jnp.concatenate([pp(from_partner[:h], right), pp(from_partner[h:], left)])
+    return mine, b, c, a, lbar, rbar, far, farbar
+
+
+def _section_reduce(parts, perms):
+    right, left, partner = perms
+    pp = lambda v, p: lax.ppermute(v, "section", p)
+    f32 = lambda v: v.astype(jnp.float32)
+    bf = lambda v: v.astype(jnp.bfloat16)
+    pm, pb, pc, pa, plbar, prbar, pfar, pfarbar = parts
+    h = pm.shape[0] // 2
+    lbar_p = f32(plbar[:h]) + f32(pp(pfarbar[:h], left))
+    rbar_q = f32(prbar[h:]) + f32(pp(pfarbar[h:], right))
+    to_left = jnp.concatenate([plbar[h:], pfar[:h]])
+    to_right = jnp.concatenate([prbar[:h], pfar[h:]])
+    to_partner = jnp.concatenate([bf(lbar_p), bf(rbar_q)])
+    got_right = f32(pp(to_left, left))
+    got_left = f32(pp(to_right, right))
+    got_partner = f32(pp(to_partner, partner))
+    pa_sum = f32(pa) + jnp.concatenate([got_left[:h], got_right[:h]])
+    pb_sum = f32(pb) + jnp.concatenate(
+        [got_right[h:] + got_partner[:h], jnp.zeros_like(got_right[h:])]
+    )
+    pc_sum = f32(pc) + jnp.concatenate(
+        [jnp.zeros_like(got_left[h:]), got_left[h:] + got_partner[h:]]
+    )
+    total = (
+        f32(pm)
+        + f32(pp(bf(pb_sum), left))
+        + f32(pp(bf(pc_sum), right))
+        + f32(pp(bf(pa_sum), partner))
+    )
+    return bf(total)
+
+
+def per_device(n_sec, tokens, expert_ids, slot_ids, router, w_in, w_out):
     tok_rows, width_model = tokens.shape
     experts = router.shape[1]
     capacity = 5 * tok_rows // (4 * experts)
+    perms = _neighbour_perms(n_sec)
     expert_hit = expert_ids[None, :] == jnp.arange(experts, dtype=jnp.int32)[:, None]
     onehots = [
         (expert_hit & (slot_ids[None, :] == c)).astype(jnp.bfloat16) for c in range(capacity)
@@ -22,19 +87,29 @@
     inward = w_in[0]
     outward = w_out[0]
     routed = lax.all_to_all(dispatch, "expert", split_axis=0, concat_axis=0, tiled=True)
-    arrived = lax.all_gather(routed, "section", axis=0, tiled=True)
-    outs = []
-    for c in range(capacity):
-        rows = arrived[:, c * width_model : (c + 1) * width_model]
-        hidden = jax.nn.relu(
-            jnp.dot(rows, inward, preferred_element_type=jnp.float32)
-        ).astype(jnp.bfloat16)
-        outs.append(
-            jnp.dot(hidden, outward, preferred_element_type=jnp.float32).astype(jnp.bfloat16)
-        )
-    summed = lax.psum_scatter(
-        jnp.concatenate(outs, axis=1), "section", scatter_dimension=0, tiled=True
-    )
+    shards = _section_gather(routed, perms)
+
+    def expert_ffn(rows_all):
+        outs = []
+        for c in range(capacity):
+            rows = rows_all[:, c * width_model : (c + 1) * width_model]
+            hidden = jax.nn.relu(
+                jnp.dot(rows, inward, preferred_element_type=jnp.float32)
+            ).astype(jnp.bfloat16)
+            outs.append(
+                jnp.dot(hidden, outward, preferred_element_type=jnp.float32).astype(
+                    jnp.bfloat16
+                )
+            )
+        return jnp.concatenate(outs, axis=1)
+
+    n = routed.shape[0]
+    near = expert_ffn(jnp.concatenate(shards[:4]))
+    away = expert_ffn(jnp.concatenate(shards[4:]))
+    parts = [near[i * n : (i + 1) * n] for i in range(4)] + [
+        away[i * n : (i + 1) * n] for i in range(4)
+    ]
+    summed = _section_reduce(parts, perms)
     returned = lax.all_to_all(summed, "expert", split_axis=0, concat_axis=0, tiled=True)
     combined = None
     for c in range(capacity):
@@ -53,8 +128,9 @@
 
 
 def solution(mesh):
+    n_sec = mesh.shape["section"]
     return jax.shard_map(
-        per_device,
+        lambda *args: per_device(n_sec, *args),
         mesh=mesh,
         in_specs=(
             P(("section", "expert"), None),

time: 398 us -> 359 us (0.902); the launches traced: 397 us -> 352 us
  waiting for transfers between devices: 257 us -> 128 us
  matrix products: 42.4 us -> 82.3 us
  starting transfers between devices: 10.2 us -> 36.3 us
  other arithmetic: 6.69 us -> 22.5 us
  local copies, waits for them, and re-layouts: 19.5 us -> 35.1 us
  between operations: 13.6 us -> 0.7 us
    reduce_scatter x1 -> x0, waiting for transfers between devices: 114 us -> none  [per_device(): lax.psum_scatter(jnp.concatenate(outs, axis=1), 'section', scatter_dimens...]
    all_gather x1 -> x0, waiting for transfers between devices: 110 us -> none  [per_device(): arrived = lax.all_gather(routed, 'section', axis=0, tiled=True)]
    ppermute x0 -> x16, waiting for transfers between devices: none -> 94.7 us  [the longest x8 65.7 us: _section_reduce(): pp = lambda v, p: lax.ppermute(v, 'section', p)]
    dot_general x10, matrix products: 32.4 us -> 72.3 us  [expert_ffn(): jnp.dot(hidden, outward, preferred_element_type=jnp.float32)]
    ppermute x0 -> x16, starting transfers between devices: none -> 17 us  [the longest x8 9.92 us: _section_gather(): pp = lambda v, p: lax.ppermute(v, 'section', p)]
    unnamed x25 -> x22, local copies, waits for them, and re-layouts: 14.8 us -> 29 us
    all_to_all x1, starting transfers between devices: 9.93 us -> 19.3 us  [per_device(): lax.all_to_all(summed, 'expert', split_axis=0, concat_axis=0, tiled=True)]
    concatenate x0 -> x5, other arithmetic: none -> 8.43 us  [the longest x1 2.83 us: per_device(): near = expert_ffn(jnp.concatenate(shards[:4]))]
  transfers between devices with their start and end apart: 3 -> 17, of which waited for: 3 -> 8; matrix products, arithmetic and copies ran while one was open for 0% -> 16% of each run, Pallas kernels for 0% -> 0%
where the time goes in v4:
time: 359 us; the launch traced here: 352 us
  waiting for transfers between devices  128 us (36%)
  matrix products  82.3 us (23%)
  blocking collectives  47.5 us (13%)
  starting transfers between devices  36.3 us (10%)
  local copies, waits for them, and re-layouts  35.1 us (10%)
  other arithmetic  22.5 us (6%)
    dot_general x10, matrix products, expert_ffn(): jnp.dot(hidden, outward, preferred_element_type=jnp.float32)  72.3 us
    ppermute x8, waiting for transfers between devices, _section_reduce(): pp = lambda v, p: lax.ppermute(v, 'section', p)  65.7 us
    all_to_all x1, blocking collectives, per_device(): lax.all_to_all(dispatch, 'expert', split_axis=0, concat_axis=0, tiled=True)  47.5 us
    all_to_all x1, waiting for transfers between devices, per_device(): lax.all_to_all(summed, 'expert', split_axis=0, concat_axis=0, tiled=True)  33.1 us
    ppermute x8, waiting for transfers between devices, _section_gather(): pp = lambda v, p: lax.ppermute(v, 'section', p)  29.1 us
    unnamed x22, local copies, waits for them, and re-layouts  29 us
    all_to_all x1, starting transfers between devices, per_device(): lax.all_to_all(summed, 'expert', split_axis=0, concat_axis=0, tiled=True)  19.3 us
    ppermute x8, starting transfers between devices, _section_gather(): pp = lambda v, p: lax.ppermute(v, 'section', p)  9.92 us
  transfers between devices with their start and end apart: 17, of which 8 were waited for; matrix products, arithmetic and copies ran while one was open for 16% of the time, Pallas kernels for 0%

profile of v4, /device:TPU:1, one launch (start us, length us, event | category | flops | bytes accessed | tf_op | source)
XLA Modules:
  0.0 352.3 jit_solution(17532849651612303018)
XLA Ops:
  7.9 3.0 reduce
  12.7 47.5 %all_to_all.24 = bf16[32,2,10240]{2,1,0:T(2,128)(2,1)S(1)} all-to-all(bf16[32,2,10240]{2,1,0:T(2,128)(2,1)} %reshape.21), channel_id=1, replica_groups=mesh['section'=8,'expert'=32] {'expert'}, dimensions={0} | all-to-all | bytes 2621440 | tf_op jit(solution)/shard_map/all_to_all | solution.py:89
  60.2 3.7 %reshape.22 = bf16[32,1,20480]{2,1,0:T(2,128)(2,1)} reshape(bf16[32,2,10240]{2,1,0:T(2,128)(2,1)S(1)} %all_to_all.24) | data formatting | bytes 2621440
  63.9 3.2 copy.16
  70.3 25.7 %collective-permute-done.2 = bf16[32,20480]{1,0:T(8,128)(2,1)S(1)} collective-permute-done((bf16[32,20480]{1,0:T(8,128)(2,1)S(1)}, bf16[32,20480]{1,0:T(8,128)(2,1)S(1)}, u32[]{:S(2)}, u32[]{:S(2)}) %collective-permute-start.2) | collective-permute-done | bytes 1310752 | tf_op jit(solution)/shard_map/ppermute | solution.py:22
  97.4 2.0 pad_maximum_fusion.1
  103.3 2.8 pad_maximum_fusion
  106.1 7.2 %fusion.45 = bf16[128,20480]{1,0:T(8,128)(2,1)} fusion(bf16[1,640,4096]{2,1,0:T(8,128)(2,1)} %param.11, bf16[1,4096,640]{2,1,0:T(8,128)(2,1)} %param.10, bf16[128,20480]{1,0:T(8,128)(2,1)} %pad_maximum_fusion), kind=kOutput, calls=%fused_computation.48 | convolution fusion | flops 1342865408 | bytes 12582912 | tf_op jit(solution)/shard_map/dot_general | solution.py:100
  113.4 7.2 %fusion.51 = bf16[128,20480]{1,0:T(8,128)(2,1)} fusion(bf16[128,20480]{1,0:T(8,128)(2,1)} %fusion.45, bf16[1,640,4096]{2,1,0:T(8,128)(2,1)} %param.11, bf16[1,4096,640]{2,1,0:T(8,128)(2,1)} %param.10, bf16[128,20480]{1,0:T(8,128)(2,1)} %pad_maximum_fusion), kind=kOutput, calls=%fused_computation.50 | convolution fusion | flops 1342865408 | bytes 12582912 | tf_op jit(solution)/shard_map/dot_general | solution.py:100
  120.6 7.2 %fusion.57 = bf16[128,20480]{1,0:T(8,128)(2,1)} fusion(bf16[128,20480]{1,0:T(8,128)(2,1)} %fusion.51, bf16[1,640,4096]{2,1,0:T(8,128)(2,1)} %param.11, bf16[1,4096,640]{2,1,0:T(8,128)(2,1)} %param.10, bf16[128,20480]{1,0:T(8,128)(2,1)} %pad_maximum_fusion), kind=kOutput, calls=%fused_computation.52 | convolution fusion | flops 1342865408 | bytes 12582912 | tf_op jit(solution)/shard_map/dot_general | solution.py:100
  128.9 2.8 collective-permute-start.7
  131.7 2.0 slice_dynamic-update-slice_fusion.3
  133.7 2.0 slice_dynamic-update-slice_fusion.2
  136.5 2.0 slice_dynamic-update-slice_fusion.1
  138.5 2.0 slice_dynamic-update-slice_fusion
  140.6 2.1 collective-permute-done.6
  144.5 7.2 %fusion.75 = bf16[128,20480]{1,0:T(8,128)(2,1)} fusion(bf16[1,640,4096]{2,1,0:T(8,128)(2,1)} %param.11, bf16[1,4096,640]{2,1,0:T(8,128)(2,1)} %param.10, bf16[128,20480]{1,0:T(8,128)(2,1)} %constant_dynamic-update-slice_fusion), kind=kOutput, calls=%fused_computation.58 | convolution fusion | flops 1342865408 | bytes 12582912 | tf_op jit(solution)/shard_map/dot_general | solution.py:100
  151.7 7.2 %fusion.81 = bf16[128,20480]{1,0:T(8,128)(2,1)} fusion(bf16[128,20480]{1,0:T(8,128)(2,1)} %fusion.75, bf16[1,640,4096]{2,1,0:T(8,128)(2,1)} %param.11, bf16[1,4096,640]{2,1,0:T(8,128)(2,1)} %param.10, bf16[128,20480]{1,0:T(8,128)(2,1)} %constant_dynamic-update-slice_fusion), kind=kOutput, calls=%fused_computation.60 | convolution fusion | flops 1342865408 | bytes 12582912 | tf_op jit(solution)/shard_map/dot_general | solution.py:100
  158.9 7.3 %fusion.87 = bf16[128,20480]{1,0:T(8,128)(2,1)} fusion(bf16[128,20480]{1,0:T(8,128)(2,1)} %fusion.81, bf16[1,640,4096]{2,1,0:T(8,128)(2,1)} %param.11, bf16[1,4096,640]{2,1,0:T(8,128)(2,1)} %param.10, bf16[128,20480]{1,0:T(8,128)(2,1)} %constant_dynamic-update-slice_fusion), kind=kOutput, calls=%fused_computation.62 | convolution fusion | flops 1342865408 | bytes 12582912 | tf_op jit(solution)/shard_map/dot_general | solution.py:100
  166.2 7.2 %fusion.93 = bf16[128,20480]{1,0:T(8,128)(2,1)} fusion(bf16[128,20480]{1,0:T(8,128)(2,1)} %fusion.87, bf16[1,640,4096]{2,1,0:T(8,128)(2,1)} %param.11, bf16[1,4096,640]{2,1,0:T(8,128)(2,1)} %param.10, bf16[128,20480]{1,0:T(8,128)(2,1)} %constant_dynamic-update-slice_fusion), kind=kOutput, calls=%fused_computation.64 | convolution fusion | flops 1342865408 | bytes 12582912 | tf_op jit(solution)/shard_map/dot_general | solution.py:100
  173.4 7.2 %fusion.99 = bf16[128,20480]{1,0:T(8,128)(2,1)} fusion(bf16[128,20480]{1,0:T(8,128)(2,1)} %fusion.93, bf16[1,640,4096]{2,1,0:T(8,128)(2,1)} %param.11, bf16[1,4096,640]{2,1,0:T(8,128)(2,1)} %param.10, bf16[128,20480]{1,0:T(8,128)(2,1)} %constant_dynamic-update-slice_fusion), kind=kOutput, calls=%fused_computation.66 | convolution fusion | flops 1342865408 | bytes 12582912 | tf_op jit(solution)/shard_map/dot_general | solution.py:100
  180.6 2.3 fusion.281
  189.8 35.7 %collective-permute-done.10 = bf16[16,20480]{1,0:T(8,128)(2,1)S(1)} collective-permute-done((bf16[16,20480]{1,0:T(8,128)(2,1)S(1)}, bf16[16,20480]{1,0:T(8,128)(2,1)S(1)}, u32[]{:S(2)}, u32[]{:S(2)}) %collective-permute-start.10) | collective-permute-done | bytes 655392 | tf_op jit(solution)/shard_map/ppermute | solution.py:42
  228.8 7.2 %fusion.63 = bf16[128,20480]{1,0:T(8,128)(2,1)} fusion(bf16[128,20480]{1,0:T(8,128)(2,1)} %fusion.57, bf16[1,640,4096]{2,1,0:T(8,128)(2,1)} %param.11, bf16[1,4096,640]{2,1,0:T(8,128)(2,1)} %param.10, bf16[128,20480]{1,0:T(8,128)(2,1)} %pad_maximum_fusion), kind=kOutput, calls=%fused_computation.54 | convolution fusion | flops 1342865408 | bytes 12582912 | tf_op jit(solution)/shard_map/dot_general | solution.py:100
  236.1 7.2 %fusion.69 = bf16[128,20480]{1,0:T(8,128)(2,1)} fusion(bf16[128,20480]{1,0:T(8,128)(2,1)} %fusion.63, bf16[1,640,4096]{2,1,0:T(8,128)(2,1)} %param.11, bf16[1,4096,640]{2,1,0:T(8,128)(2,1)} %param.10, bf16[128,20480]{1,0:T(8,128)(2,1)} %pad_maximum_fusion), kind=kOutput, calls=%fused_computation.56 | convolution fusion | flops 1342865408 | bytes 12582912 | tf_op jit(solution)/shard_map/dot_general | solution.py:100
  246.2 7.2 %collective-permute-done.11 = bf16[32,20480]{1,0:T(8,128)(2,1)} collective-permute-done((bf16[32,20480]{1,0:T(8,128)(2,1)}, bf16[32,20480]{1,0:T(8,128)(2,1)}, u32[]{:S(2)}, u32[]{:S(2)}) %collective-permute-start.11) | collective-permute-done | bytes 1310752 | tf_op jit(solution)/shard_map/ppermute | solution.py:42
  259.3 21.9 %collective-permute-done.12 = bf16[32,20480]{1,0:T(8,128)(2,1)S(1)} collective-permute-done((bf16[32,20480]{1,0:T(8,128)(2,1)S(1)}, bf16[32,20480]{1,0:T(8,128)(2,1)S(1)}, u32[]{:S(2)}, u32[]{:S(2)}) %collective-permute-start.12) | collective-permute-done | bytes 1310752 | tf_op jit(solution)/shard_map/ppermute | solution.py:42
  283.8 3.0 reduce.1
  288.6 19.3 %all-to-all-start.1 = ((bf16[32,2,10240]{2,1,0:T(2,128)(2,1)}), bf16[32,2,10240]{2,1,0:T(2,128)(2,1)S(1)}, u32[]{:S(2)}, u32[]{:S(2)}) async-start(bf16[32,2,10240]{2,1,0:T(2,128)(2,1)} %reshape.23), calls=%async_computation.1 | async-start | bytes 2621440 | tf_op jit(solution)/shard_map/all_to_all | solution.py:113
  308.4 33.1 %all-to-all-done.1 = bf16[32,2,10240]{2,1,0:T(2,128)(2,1)S(1)} async-done(((bf16[32,2,10240]{2,1,0:T(2,128)(2,1)}), bf16[32,2,10240]{2,1,0:T(2,128)(2,1)S(1)}, u32[]{:S(2)}, u32[]{:S(2)}) %all-to-all-start.1) | async-done | bytes 1310752 | tf_op jit(solution)/shard_map/all_to_all | solution.py:113
  341.4 3.7 %reshape.24 = bf16[32,1,20480]{2,1,0:T(2,128)(2,1)} reshape(bf16[32,2,10240]{2,1,0:T(2,128)(2,1)S(1)} %all-to-all-done.1) | data formatting | bytes 2621440
  345.2 3.2 copy.15
  (72 shorter events, 49.2 us)
Async XLA Ops:
  0.0 1.2 copy-start
  0.0 4.5 %copy-start.2 = (s32[128]{0:T(128)S(1)}, s32[128]{0:T(128)}, u32[]{:S(2)}) copy-start(s32[128]{0:T(128)} %param.7) | copy-start | bytes 1540
  67.1 28.9 %collective-permute-start.2 = (bf16[32,20480]{1,0:T(8,128)(2,1)S(1)}, bf16[32,20480]{1,0:T(8,128)(2,1)S(1)}, u32[]{:S(2)}, u32[]{:S(2)}) collective-permute-start(bf16[32,20480]{1,0:T(8,128)(2,1)S(1)} %bitcast.160), channel_id=1, source_target_pairs={{0,128},{32,160},{64,192},{96,224},{128,0},{160,32},{192,64},{224,... | collective-permute-start | bytes 3932168 | tf_op jit(solution)/shard_map/ppermute | solution.py:22
  67.6 29.7 %collective-permute-start = (bf16[32,20480]{1,0:T(8,128)(2,1)S(1)}, bf16[32,20480]{1,0:T(8,128)(2,1)S(1)}, u32[]{:S(2)}, u32[]{:S(2)}) collective-permute-start(bf16[32,20480]{1,0:T(8,128)(2,1)S(1)} %bitcast.161), channel_id=1, source_target_pairs={{0,32},{32,64},{64,96},{96,0},{128,160},{160,192},{192,224},{224,1... | collective-permute-start | bytes 3932168 | tf_op jit(solution)/shard_map/ppermute | solution.py:22
  68.8 28.5 %collective-permute-start.1 = (bf16[32,20480]{1,0:T(8,128)(2,1)S(1)}, bf16[32,20480]{1,0:T(8,128)(2,1)S(1)}, u32[]{:S(2)}, u32[]{:S(2)}) collective-permute-start(bf16[32,20480]{1,0:T(8,128)(2,1)S(1)} %bitcast.162), channel_id=1, source_target_pairs={{0,96},{32,0},{64,32},{96,64},{128,224},{160,128},{192,160},{224,1... | collective-permute-start | bytes 3932168 | tf_op jit(solution)/shard_map/ppermute | solution.py:22
  99.4 28.4 %collective-permute-start.3 = (bf16[32,20480]{1,0:T(8,128)(2,1)}, bf16[32,20480]{1,0:T(8,128)(2,1)S(1)}, u32[]{:S(2)}, u32[]{:S(2)}) collective-permute-start(bf16[32,20480]{1,0:T(8,128)(2,1)} %get-tuple-element.24), channel_id=1, source_target_pairs={{0,128},{32,160},{64,192},{96,224},{128,0},{160,32},{192,64},{224,... | collective-permute-start | bytes 3932168 | tf_op jit(solution)/shard_map/ppermute | solution.py:22
  100.5 31.2 %collective-permute-start.4 = (bf16[32,20480]{1,0:T(8,128)(2,1)}, bf16[32,20480]{1,0:T(8,128)(2,1)}, u32[]{:S(2)}, u32[]{:S(2)}) collective-permute-start(bf16[32,20480]{1,0:T(8,128)(2,1)} %get-tuple-element.25), channel_id=1, source_target_pairs={{0,32},{32,64},{64,96},{96,0},{128,160},{160,192},{192,224},{224,1... | collective-permute-start | bytes 3932168 | tf_op jit(solution)/shard_map/ppermute | solution.py:22
  101.4 32.3 %collective-permute-start.5 = (bf16[32,20480]{1,0:T(8,128)(2,1)}, bf16[32,20480]{1,0:T(8,128)(2,1)}, u32[]{:S(2)}, u32[]{:S(2)}) collective-permute-start(bf16[32,20480]{1,0:T(8,128)(2,1)} %get-tuple-element.23), channel_id=1, source_target_pairs={{0,96},{32,0},{64,32},{96,64},{128,224},{160,128},{192,160},{224,1... | collective-permute-start | bytes 3932168 | tf_op jit(solution)/shard_map/ppermute | solution.py:22
  128.8 13.9 %collective-permute-start.6 = (bf16[16,20480]{1,0:T(8,128)(2,1)S(1)}, bf16[16,20480]{1,0:T(8,128)(2,1)S(1)}, u32[]{:S(2)}, u32[]{:S(2)}) collective-permute-start(bf16[16,20480]{1,0:T(8,128)(2,1)S(1)} %get-tuple-element.20), channel_id=1, source_target_pairs={{0,32},{32,64},{64,96},{96,0},{128,160},{160,192},{192,224},{224,1... | collective-permute-start | bytes 1966088 | tf_op jit(solution)/shard_map/ppermute | solution.py:22
  128.9 14.7 %collective-permute-start.7 = (bf16[16,20480]{1,0:T(8,128)(2,1)S(1)}, bf16[16,20480]{1,0:T(8,128)(2,1)S(1)}, u32[]{:S(2)}, u32[]{:S(2)}) collective-permute-start(bf16[16,20480]{1,0:T(8,128)(2,1)S(1)} %get-tuple-element.18), channel_id=1, source_target_pairs={{0,96},{32,0},{64,32},{96,64},{128,224},{160,128},{192,160},{224,1... | collective-permute-start | bytes 1966088 | tf_op jit(solution)/shard_map/ppermute | solution.py:22
  184.2 59.1 %collective-permute-start.13 = (bf16[32,20480]{1,0:T(8,128)(2,1)}, bf16[32,20480]{1,0:T(8,128)(2,1)S(1)}, u32[]{:S(2)}, u32[]{:S(2)}) collective-permute-start(bf16[32,20480]{1,0:T(8,128)(2,1)} %pad_maximum_fusion.6), channel_id=1, source_target_pairs={{0,32},{32,64},{64,96},{96,0},{128,160},{160,192},{192,224},{224,1... | collective-permute-start | bytes 3932168 | tf_op jit(solution)/shard_map/ppermute | solution.py:42
  184.4 41.1 %collective-permute-start.10 = (bf16[16,20480]{1,0:T(8,128)(2,1)S(1)}, bf16[16,20480]{1,0:T(8,128)(2,1)S(1)}, u32[]{:S(2)}, u32[]{:S(2)}) collective-permute-start(bf16[16,20480]{1,0:T(8,128)(2,1)S(1)} %get-tuple-element.13), channel_id=1, source_target_pairs={{0,32},{32,64},{64,96},{96,0},{128,160},{160,192},{192,224},{224,1... | collective-permute-start | bytes 1966088 | tf_op jit(solution)/shard_map/ppermute | solution.py:42
  185.7 39.8 %collective-permute-start.9 = (bf16[16,20480]{1,0:T(8,128)(2,1)S(1)}, bf16[16,20480]{1,0:T(8,128)(2,1)S(1)}, u32[]{:S(2)}, u32[]{:S(2)}) collective-permute-start(bf16[16,20480]{1,0:T(8,128)(2,1)S(1)} %get-tuple-element.10), channel_id=1, source_target_pairs={{0,96},{32,0},{64,32},{96,64},{128,224},{160,128},{192,160},{224,1... | collective-permute-start | bytes 1966088 | tf_op jit(solution)/shard_map/ppermute | solution.py:42
  188.3 55.3 %collective-permute-start.8 = (bf16[32,20480]{1,0:T(8,128)(2,1)}, bf16[32,20480]{1,0:T(8,128)(2,1)}, u32[]{:S(2)}, u32[]{:S(2)}) collective-permute-start(bf16[32,20480]{1,0:T(8,128)(2,1)} %pad_maximum_fusion.4), channel_id=1, source_target_pairs={{0,96},{32,0},{64,32},{96,64},{128,224},{160,128},{192,160},{224,1... | collective-permute-start | bytes 3932168 | tf_op jit(solution)/shard_map/ppermute | solution.py:42
  228.2 25.2 %collective-permute-start.11 = (bf16[32,20480]{1,0:T(8,128)(2,1)}, bf16[32,20480]{1,0:T(8,128)(2,1)}, u32[]{:S(2)}, u32[]{:S(2)}) collective-permute-start(bf16[32,20480]{1,0:T(8,128)(2,1)} %pad_maximum_fusion.5), channel_id=1, source_target_pairs={{0,128},{32,160},{64,192},{96,224},{128,0},{160,32},{192,64},{224,... | collective-permute-start | bytes 3932168 | tf_op jit(solution)/shard_map/ppermute | solution.py:42
  253.4 2.6 slice-start
  255.1 1.5 slice-start.1
  257.1 24.0 %collective-permute-start.12 = (bf16[32,20480]{1,0:T(8,128)(2,1)S(1)}, bf16[32,20480]{1,0:T(8,128)(2,1)S(1)}, u32[]{:S(2)}, u32[]{:S(2)}) collective-permute-start(bf16[32,20480]{1,0:T(8,128)(2,1)S(1)} %get-tuple-element.5), channel_id=1, source_target_pairs={{0,96},{32,0},{64,32},{96,64},{128,224},{160,128},{192,160},{224,1... | collective-permute-start | bytes 3932168 | tf_op jit(solution)/shard_map/ppermute | solution.py:42
  257.3 24.7 %collective-permute-start.14 = (bf16[32,20480]{1,0:T(8,128)(2,1)S(1)}, bf16[32,20480]{1,0:T(8,128)(2,1)S(1)}, u32[]{:S(2)}, u32[]{:S(2)}) collective-permute-start(bf16[32,20480]{1,0:T(8,128)(2,1)S(1)} %get-tuple-element.7), channel_id=1, source_target_pairs={{0,32},{32,64},{64,96},{96,0},{128,160},{160,192},{192,224},{224,1... | collective-permute-start | bytes 3932168 | tf_op jit(solution)/shard_map/ppermute | solution.py:42
  258.7 23.4 %collective-permute-start.15 = (bf16[32,20480]{1,0:T(8,128)(2,1)S(1)}, bf16[32,20480]{1,0:T(8,128)(2,1)S(1)}, u32[]{:S(2)}, u32[]{:S(2)}) collective-permute-start(bf16[32,20480]{1,0:T(8,128)(2,1)S(1)} %get-tuple-element.6), channel_id=1, source_target_pairs={{0,128},{32,160},{64,192},{96,224},{128,0},{160,32},{192,64},{224,... | collective-permute-start | bytes 3932168 | tf_op jit(solution)/shard_map/ppermute | solution.py:42
  286.7 21.1 %copy-start.1 = (bf16[4096,32]{0,1:T(8,128)(2,1)S(1)}, bf16[4096,32]{0,1:T(8,128)(2,1)}, u32[]{:S(2)}) copy-start(bf16[4096,32]{0,1:T(8,128)(2,1)} %param.9) | copy-start | bytes 786436
  288.6 52.9 %all-to-all-start.1 = ((bf16[32,2,10240]{2,1,0:T(2,128)(2,1)}), bf16[32,2,10240]{2,1,0:T(2,128)(2,1)S(1)}, u32[]{:S(2)}, u32[]{:S(2)}) async-start(bf16[32,2,10240]{2,1,0:T(2,128)(2,1)} %reshape.23), calls=%async_computation.1 | async-start | bytes 2621440 | tf_op jit(solution)/shard_map/all_to_all | solution.py:113
